TPU v7x, 128 devices: a whole 4x4x4 slice. The times are simulated.
128 devices in a mesh: chaos: 8 (over x, y_hi), space: 16 (over y_lo, z, core).
Axes of the slice: x: 4, y: 4 (y_hi: 2, y_lo: 2; y = y_hi * 2 + y_lo), z: 4, core: 2. Of those that a mesh axis runs over, the one named last changes fastest.
Arguments:
- modes: float32 [120, 128, 2048], P('chaos', 'space'), may hold values from -2 to 2
- kl_fields: float32 [8, 128, 2048], P(None, 'space'), may hold values from 0.1 to 1
- triples: int32 [624, 3], replicated, may hold values from 0 to 119, as said below
- ratios: int32 [624, 2], replicated, may hold values from 1 to 12, as said below
- mode_of_slot: int32 [120], replicated, may hold values from 0 to 119, each once
Outputs:
- applied: float32 [120, 128, 2048], P('chaos', 'space')
Inputs may be any that keep to these rules, and one draw needn't show every extreme that they name: `triples`: rows are distinct. Modes are the multi-indices of total degree at most 3 in 7 variables. Every mode i has the row (i, i, 0); every other row (i, j, k) has k of 1 or more, and the multi-indices of i and j differ by one in variable k and agree elsewhere; each such pair appears in both orders. `ratios`: column 0 is a positive numerator, column 1 a denominator of 1 to 4. `mode_of_slot`: A permutation.
All inputs are finite; a program needn't handle non-finite values.
Results may differ from a plain program's by a relative error of at most 0.000082.
Values sent between devices are 32-bit elements; how exact they have to be, the bound alone decides.
No kernel may reach another device: no remote copies, remote signals or barrier semaphores. Data moves between devices by JAX's collectives and lax.ppermute only.
A program may use at most 128 MiB of HBM per device.

v0:
```python
import jax
import jax.numpy as jnp
from jax import lax
from jax.sharding import PartitionSpec as P


def extended_2(x, sides, width):
    for axis, dim in sides:
        count, length = (lax.axis_size(axis), x.shape[dim])
        up = [(i, (i + 1) % count) for i in range(count - 1)]
        down = [(j, i) for i, j in up]
        last = lax.slice_in_dim(x, length - width, length, axis=dim)
        first = lax.slice_in_dim(x, 0, width, axis=dim)
        before = lax.ppermute(last, axis, up)
        after = lax.ppermute(first, axis, down)
        x = jnp.concatenate([before, x, after], axis=dim)
    return x


def shift_cols(x, direction):
    zero = jnp.zeros_like(x[..., :1])
    if direction > 0:
        return jnp.concatenate([zero, x[..., :-1]], axis=-1)
    return jnp.concatenate([x[..., 1:], zero], axis=-1)


def coupling_table(triples, ratios, mode_of_slot, kl_terms, mode_count):
    matches = triples[:, :2, None] == mode_of_slot[None, None, :]
    slot_pairs = jnp.sum(jnp.where(matches, jnp.arange(mode_count, dtype=jnp.int32), 0), axis=2)
    weights = ratios[:, 0].astype(jnp.float32) / ratios[:, 1].astype(jnp.float32)
    flat_index = (triples[:, 2] * mode_count + slot_pairs[:, 0]) * mode_count + slot_pairs[:, 1]
    coupling = (
        jnp.zeros((kl_terms * mode_count * mode_count,), jnp.float32).at[flat_index].add(weights)
    )
    return coupling.reshape(kl_terms, mode_count, mode_count)


def neighbour_table(local_rows):
    mode_count = local_rows.shape[-1]
    present = local_rows > 0
    first = jnp.argmax(present, axis=-1).astype(jnp.int32)
    last = (mode_count - 1 - jnp.argmax(present[..., ::-1], axis=-1)).astype(jnp.int32)
    w_first = jnp.take_along_axis(local_rows, first[..., None], axis=-1)[..., 0]
    w_last = jnp.take_along_axis(local_rows, last[..., None], axis=-1)[..., 0]
    w_last = jnp.where(last == first, jnp.zeros_like(w_last), w_last)
    return (first, last, w_first, w_last)


def local(modes, kl_fields, triples, ratios, mode_of_slot):
    groups = lax.axis_size("chaos")
    own_modes = modes.shape[0]
    mode_count = own_modes * groups
    kl_terms = kl_fields.shape[0]
    first_slot = lax.axis_index("chaos") * own_modes
    coupling = coupling_table(triples, ratios, mode_of_slot, kl_terms, mode_count)
    local_rows = lax.dynamic_slice_in_dim(coupling, first_slot, own_modes, 1)
    first, last, w_first, w_last = neighbour_table(local_rows)
    joined = jnp.concatenate([modes, kl_fields], axis=0)
    padded = extended_2(joined, (("space", 1),), 1)
    source = padded[:own_modes]
    coef = padded[own_modes:]
    every = lax.all_gather(source, "chaos", axis=0, tiled=True)
    a_c = coef[:, 1:-1]
    c_up = (a_c + coef[:, :-2])[:, None]
    c_dn = (a_c + coef[:, 2:])[:, None]
    c_lf = (a_c + shift_cols(a_c, 1))[:, None]
    c_rt = (a_c + shift_cols(a_c, -1))[:, None]
    g_first = jnp.take(every, first.reshape(-1), axis=0).reshape(
        (kl_terms, own_modes) + every.shape[1:]
    )
    g_last = jnp.take(every, last.reshape(-1), axis=0).reshape(
        (kl_terms, own_modes) + every.shape[1:]
    )
    mixed = w_first[:, :, None, None] * g_first + w_last[:, :, None, None] * g_last
    center = mixed[:, :, 1:-1]
    result = c_up * (center - mixed[:, :, :-2])
    result = result + c_dn * (center - mixed[:, :, 2:])
    result = result + c_lf * (center - shift_cols(center, 1))
    result = result + c_rt * (center - shift_cols(center, -1))
    return 0.5 * jnp.sum(result, axis=0)


def solution(mesh):
    return jax.shard_map(
        local,
        mesh=mesh,
        in_specs=(P("chaos", "space", None), P(None, "space", None), P(), P(), P()),
        out_specs=P("chaos", "space", None),
        check_vma=False,
    )
```

profile of v0, /device:TPU:0, one launch (start us, length us, event | category | flops | bytes accessed | tf_op | source)
XLA Modules:
  0.0 301.7 jit_solution(17905389642816986577)
XLA Ops:
  6.6 1.8 copy.16
  8.4 1.4 copy.18
  9.8 1.3 collective-permute-start
  11.1 1.3 collective-permute-start.1
  12.4 4.3 %collective-permute-done.1 = f32[23,1,2048]{2,0,1:T(8,128)S(1)} collective-permute-done((f32[23,1,2048]{2,0,1:T(8,128)S(1)}, f32[23,1,2048]{2,0,1:T(8,128)S(1)}, u32[]{:S(2)}, u32[]{:S(2)}) %collective-permute-start.1) | collective-permute-done | bytes 188448 | tf_op jit(solution)/shard_map/ppermute | solution.py:15
  16.8 2.0 copy.20
  19.1 4.7 %scatter_custom_fusion = f32[115200]{0:T(1024)S(1)} fusion(s32[624]{0:T(1024)S(1)} %fusion.22, f32[624]{0:T(1024)S(1)} %fusion.24, f32[]{:T(128)} %constant.6.clone.1), kind=kCustom, calls=%fused_computation.29 | custom fusion | flops 624 | bytes 460804 | tf_op jit(solution)/shard_map/scatter-add | solution.py:33
  24.5 1.1 iota_reduce_fusion.1
  25.7 0.9 iota_reduce_fusion
  26.7 2.1 gather_fusion.2
  28.9 2.1 gather_fusion
  31.5 1.0 pad_add_fusion.1
  32.6 1.1 copy.19
  33.7 1.1 copy.22
  34.8 166.2 %all-gather.2.cloned.1.call-done = f32[120,10,2048]{2,1,0:T(8,128)} async-done(((f32[15,10,2048]{2,1,0:T(8,128)}), f32[120,10,2048]{2,1,0:T(8,128)}) %all-gather.2.cloned.1.call-update) | async-done | bytes 9830416 | tf_op jit(solution)/shard_map/all_gather | solution.py:62
  201.0 15.0 %gather_fusion.1 = f32[120,10,2048]{2,1,0:T(8,128)} fusion(f32[120,10,2048]{2,1,0:T(8,128)} %all-gather.2.cloned.1.call-done, s32[1024]{0:T(1024)S(1)} %pad_clamp_fusion.1), kind=kCustom, calls=%fused_computation.1.clone | custom fusion | bytes 19661280 | tf_op jit(solution)/shard_map/jit(_take)/gather | solution.py:68
  216.0 11.6 %broadcast_select_fusion.1 = f32[120,10,2048]{2,1,0:T(8,128)} fusion(f32[120,10,2048]{2,1,0:T(8,128)} %gather_fusion.1, pred[120]{0:T(512)(128)(4,1)S(1)} %compare_and_fusion.1), kind=kLoop, calls=%fused_computation.15 | loop fusion | flops 2457600 | bytes 19660920 | tf_op jit(solution)/shard_map/jit(_take)/select_n | solution.py:68
  227.7 15.0 %gather_fusion.3 = f32[120,10,2048]{2,1,0:T(8,128)} fusion(f32[120,10,2048]{2,1,0:T(8,128)} %all-gather.2.cloned.1.call-done, s32[1024]{0:T(1024)S(1)} %pad_clamp_fusion), kind=kCustom, calls=%fused_computation.3.clone | custom fusion | bytes 19661280 | tf_op jit(solution)/shard_map/jit(_take)/gather | solution.py:71
  242.7 6.8 %broadcast_select_fusion = f32[120,10,2048]{2,1,0:T(8,128)S(1)} fusion(f32[120,10,2048]{2,1,0:T(8,128)} %gather_fusion.3, pred[120]{0:T(512)(128)(4,1)S(1)} %compare_and_fusion), kind=kLoop, calls=%fused_computation.14 | loop fusion | flops 2457600 | bytes 19660920 | tf_op jit(solution)/shard_map/jit(_take)/select_n | solution.py:71
  249.6 3.2 %copy-done = f32[120,10,2048]{2,1,0:T(8,128)S(1)} copy-done((f32[120,10,2048]{2,1,0:T(8,128)S(1)}, f32[120,10,2048]{2,1,0:T(8,128)}, u32[]{:S(2)}) %copy-start) | copy-done | bytes 9830424
  252.7 7.1 %multiply_add_fusion = f32[8,15,10,2048]{3,2,1,0:T(8,128)} fusion(f32[8,15,10,2048]{3,2,1,0:T(8,128)S(1)} %bitcast.31, f32[8,15,10,2048]{3,2,1,0:T(8,128)S(1)} %bitcast.30, f32[8,15]{1,0:T(8,128)S(1)} %bitcast_select_fusion, f32[8,15]{1,0:T(8,128)S(1)} %select_bitcast_fusion), kind=kLoop, calls=%fused_computation.5 | loop fusion | flops 7372800 | bytes 29492160 | tf_op jit(solution)/shard_map/add | solution.py:74
  259.8 15.7 %fusion.25 = (f32[8,15,8,2047]{3,2,1,0:T(8,128)S(1)}, f32[8,15,8,2047]{3,2,1,0:T(8,128)}) fusion(f32[8,15,10,2048]{3,2,1,0:T(8,128)} %multiply_add_fusion), kind=kLoop, calls=%fused_computation.76 | loop fusion | bytes 31441920 | tf_op jit(solution)/shard_map/slice | solution.py:23
  275.5 18.3 %fusion.4 = f32[15,8,2048]{2,1,0:T(8,128)S(1)} fusion(f32[8,15,10,2048]{3,2,1,0:T(8,128)} %multiply_add_fusion, f32[8,15,8,2047]{3,2,1,0:T(8,128)} %get-tuple-element.14, f32[8,15,8,2047]{3,2,1,0:T(8,128)S(1)} %get-tuple-element.13, f32[8,8,2048]{2,1,0:T(8,128)} %get-tuple-element.20, f32[8,8,2048]{2,1,0:T(8,128)S(1)} %get-tuple-element.19, ...), kind=kLoop, calls=%fused_computation.11 | loop fusion | flops 23347200 | bytes 42394112 | tf_op jit(solution)/shard_map/reduce_sum | solution.py:80
  293.8 1.1 broadcast_multiply_fusion
  (49 shorter events, 2.0 us)
Async XLA Ops:
  6.5 12.3 %slice-start = ((s32[624,3]{0,1:T(4,128)}), s32[624,2]{0,1:T(2,128)S(1)}, s32[]{:S(2)}) async-start(s32[624,3]{0,1:T(4,128)} %param.11), calls=%async_computation.1 | async-start | bytes 10240 | tf_op jit(solution)/shard_map/slice | solution.py:28
  6.5 12.5 %copy-start.4 = (s32[624,3]{0,1:T(4,128)S(1)}, s32[624,3]{0,1:T(4,128)}, u32[]{:S(2)}) copy-start(s32[624,3]{0,1:T(4,128)} %param.11) | copy-start | bytes 22468
  6.5 12.3 %copy-start.6 = (s32[120]{0:T(128)S(1)}, s32[120]{0:T(128)}, u32[]{:S(2)}) copy-start(s32[120]{0:T(128)} %param.13) | copy-start | bytes 1444
  6.5 12.5 %copy-start.5 = (s32[624,2]{0,1:T(2,128)S(1)}, s32[624,2]{0,1:T(2,128)}, u32[]{:S(2)}) copy-start(s32[624,2]{0,1:T(2,128)} %param.12) | copy-start | bytes 14980
  6.5 194.5 %all-gather.2.cloned.1.call-start = ((), (), s32[]{:S(2)}) async-start(), calls=%async_computation | async-start | bytes 17694720 | tf_op jit(solution)/shard_map/all_gather | solution.py:62
  9.8 2.6 collective-permute-start
  11.1 5.6 %collective-permute-start.1 = (f32[23,1,2048]{2,0,1:T(8,128)S(1)}, f32[23,1,2048]{2,0,1:T(8,128)S(1)}, u32[]{:S(2)}, u32[]{:S(2)}) collective-permute-start(f32[23,1,2048]{2,0,1:T(8,128)S(1)} %get-tuple-element.18), channel_id=1, source_target_pairs={{1,0},{2,1},{3,2},{4,3},{5,4},{6,5},{7,6},{8,7},{9,8},{10,9},{11,1... | collective-permute-start | bytes 565256 | tf_op jit(solution)/shard_map/ppermute | solution.py:15
  16.7 2.4 copy-start.2
  16.8 14.5 %copy-start.1 = (f32[8,8,2048]{2,1,0:T(8,128)S(1)}, f32[8,8,2048]{2,1,0:T(8,128)}, u32[]{:S(2)}) copy-start(f32[8,8,2048]{2,1,0:T(8,128)} %param.10) | copy-start | bytes 1572868
  24.3 8.1 %copy-start.3 = (f32[23,1,2048]{2,0,1:T(8,128)S(1)}, f32[23,1,2048]{2,0,1:T(8,128)}, u32[]{:S(2)}) copy-start(f32[23,1,2048]{2,0,1:T(8,128)} %copy-done.2) | copy-start | bytes 565252
  242.7 10.0 %copy-start = (f32[120,10,2048]{2,1,0:T(8,128)S(1)}, f32[120,10,2048]{2,1,0:T(8,128)}, u32[]{:S(2)}) copy-start(f32[120,10,2048]{2,1,0:T(8,128)} %broadcast_select_fusion.1) | copy-start | bytes 29491204
Sparse Core Ops, SparseCore 0:
  18.9 182.0 all-gather.1
where the time goes:
time: 302 us
  waiting for transfers between devices  170 us (56%)
  local copies, waits for them, and re-layouts  61.7 us (20%)
  other arithmetic  53.2 us (18%)
  between operations  13.7 us (5%)
    all_gather x1, waiting for transfers between devices, local(): every = lax.all_gather(source, 'chaos', axis=0, tiled=True)  166 us
    reduce_sum x1, other arithmetic, local(): return 0.5 * jnp.sum(result, axis=0)  18.3 us
    slice x2, local copies, waits for them, and re-layouts, shift_cols(): return jnp.concatenate([zero, x[..., :-1]], axis=-1)  15.9 us
    gather x1, local copies, waits for them, and re-layouts, local(): jnp.take(every, last.reshape(-1), axis=0)  15 us
    gather x1, local copies, waits for them, and re-layouts, local(): jnp.take(every, first.reshape(-1), axis=0)  15 us
    select_n x2, other arithmetic, local(): jnp.take(every, first.reshape(-1), axis=0)  11.6 us
    add x1, other arithmetic, local(): w_first[:, :, None, None] * g_first + w_last[:, :, None, None] * g_last  7.05 us
    select_n x2, other arithmetic, local(): jnp.take(every, last.reshape(-1), axis=0)  6.84 us
  transfers between devices with their start and end apart: 3, of which 2 were waited for; matrix products, arithmetic and copies ran while one was open for 5% of the time, Pallas kernels for 0%

commit v1 on v0

--- a/solution.py
+++ b/solution.py
@@ -59,7 +59,9 @@
     padded = extended_2(joined, (("space", 1),), 1)
     source = padded[:own_modes]
     coef = padded[own_modes:]
-    every = lax.all_gather(source, "chaos", axis=0, tiled=True)
+    every = jnp.concatenate(
+        lax.all_to_all(jnp.stack([source] * lax.axis_size("chaos")), "chaos", 0, 0), axis=0
+    )
     a_c = coef[:, 1:-1]
     c_up = (a_c + coef[:, :-2])[:, None]
     c_dn = (a_c + coef[:, 2:])[:, None]

time: 302 us -> 273 us (0.904); the launches traced: 302 us -> 269 us
  waiting for transfers between devices: 170 us -> 132 us
  between operations: 13.7 us -> 0.28 us
  local copies, waits for them, and re-layouts: 61.7 us -> 69.2 us
  starting transfers between devices: 2.63 us -> 9.67 us
  other arithmetic: 53.2 us -> 57.5 us
    all_gather x1 -> x0, waiting for transfers between devices: 166 us -> none  [local(): every = lax.all_gather(source, 'chaos', axis=0, tiled=True)]
    all_to_all x0 -> x1, waiting for transfers between devices: none -> 128 us  [local(): lax.all_to_all(jnp.stack([source] * lax.axis_size('chaos')), 'chaos', 0, 0)]
    reshape x0 -> x1, local copies, waits for them, and re-layouts: none -> 16 us  [local(): jnp.concatenate(lax.all_to_all(jnp.stack([source] * lax.axis_size('chaos'...]
    add x1, other arithmetic: 7.05 us -> 19 us  [local(): w_first[:, :, None, None] * g_first + w_last[:, :, None, None] * g_last]
    slice x2, local copies, waits for them, and re-layouts: 15.9 us -> 5.68 us  [shift_cols(): return jnp.concatenate([zero, x[..., :-1]], axis=-1)]
    reduce_sum x1, other arithmetic: 18.3 us -> 8.79 us  [local(): return 0.5 * jnp.sum(result, axis=0)]
    all_to_all x0 -> x1, starting transfers between devices: none -> 7.07 us  [local(): lax.all_to_all(jnp.stack([source] * lax.axis_size('chaos')), 'chaos', 0, 0)]
    another operation x0 -> x1, local copies, waits for them, and re-layouts: none -> 5.31 us  [local(): jnp.stack([source] * lax.axis_size('chaos'))]
  transfers between devices with their start and end apart: 3 -> 3, of which waited for: 2 -> 2; matrix products, arithmetic and copies ran while one was open for 5% -> 6% of each run, Pallas kernels for 0% -> 0%
where the time goes in v1:
time: 273 us; the launch traced here: 269 us
  waiting for transfers between devices  132 us (48%)
  local copies, waits for them, and re-layouts  69.2 us (25%)
  other arithmetic  57.5 us (21%)
  starting transfers between devices  9.67 us (4%)
    all_to_all x1, waiting for transfers between devices, local(): lax.all_to_all(jnp.stack([source] * lax.axis_size('chaos')), 'chaos', 0, 0)  128 us
    add x1, other arithmetic, local(): w_first[:, :, None, None] * g_first + w_last[:, :, None, None] * g_last  19 us
    reshape x1, local copies, waits for them, and re-layouts, local(): jnp.concatenate(lax.all_to_all(jnp.stack([source] * lax.axis_size('chaos'...  16 us
    gather x1, local copies, waits for them, and re-layouts, local(): jnp.take(every, last.reshape(-1), axis=0)  15.3 us
    gather x1, local copies, waits for them, and re-layouts, local(): jnp.take(every, first.reshape(-1), axis=0)  15 us
    select_n x2, other arithmetic, local(): jnp.take(every, first.reshape(-1), axis=0)  12.8 us
    reduce_sum x1, other arithmetic, local(): return 0.5 * jnp.sum(result, axis=0)  8.79 us
    all_to_all x1, starting transfers between devices, local(): lax.all_to_all(jnp.stack([source] * lax.axis_size('chaos')), 'chaos', 0, 0)  7.07 us
  transfers between devices with their start and end apart: 3, of which 2 were waited for; matrix products, arithmetic and copies ran while one was open for 6% of the time, Pallas kernels for 0%

profile of v1, /device:TPU:0, one launch (start us, length us, event | category | flops | bytes accessed | tf_op | source)
XLA Modules:
  0.0 268.6 jit_solution(9394252604316788404)
XLA Ops:
  0.0 1.8 copy.60
  1.8 1.4 copy.62
  3.2 1.3 collective-permute-start
  4.5 1.3 collective-permute-start.1
  5.8 4.3 %collective-permute-done.1 = f32[23,1,2048]{2,0,1:T(8,128)S(1)} collective-permute-done((f32[23,1,2048]{2,0,1:T(8,128)S(1)}, f32[23,1,2048]{2,0,1:T(8,128)S(1)}, u32[]{:S(2)}, u32[]{:S(2)}) %collective-permute-start.1) | collective-permute-done | bytes 188448 | tf_op jit(solution)/shard_map/ppermute | solution.py:15
  10.2 5.3 %stack.2 = f32[8,15,10,2048]{3,1,2,0:T(8,128)} broadcast(f32[15,10,2048]{2,0,1:T(8,128)S(1)} %pad_maximum_fusion), dimensions={1,2,3} | broadcast | bytes 11059200 | tf_op jit(solution)/shard_map/stack | solution.py:63
  15.5 7.1 %all-to-all-start = ((f32[8,15,10,2048]{3,1,2,0:T(8,128)}), f32[8,15,10,2048]{3,1,2,0:T(8,128)}, u32[]{:S(2)}, u32[]{:S(2)}) async-start(f32[8,15,10,2048]{3,1,2,0:T(8,128)} %stack.2), calls=%async_computation | async-start | bytes 20971520 | tf_op jit(solution)/shard_map/all_to_all | solution.py:63
  22.9 4.7 %scatter_custom_fusion = f32[115200]{0:T(1024)S(1)} fusion(s32[624]{0:T(1024)S(1)} %fusion.23, f32[624]{0:T(1024)S(1)} %fusion.25, f32[]{:T(128)} %constant.6.clone.1), kind=kCustom, calls=%fused_computation.31 | custom fusion | flops 624 | bytes 460804 | tf_op jit(solution)/shard_map/scatter-add | solution.py:33
  28.2 1.1 iota_reduce_fusion.1
  29.4 0.9 iota_reduce_fusion
  30.5 2.1 gather_fusion.2
  32.7 2.1 gather_fusion
  36.1 1.8 fusion.8
  37.9 127.8 %all-to-all-done = f32[8,15,10,2048]{3,1,2,0:T(8,128)} async-done(((f32[8,15,10,2048]{3,1,2,0:T(8,128)}), f32[8,15,10,2048]{3,1,2,0:T(8,128)}, u32[]{:S(2)}, u32[]{:S(2)}) %all-to-all-start) | async-done | bytes 9830432 | tf_op jit(solution)/shard_map/all_to_all | solution.py:63
  165.7 16.0 %copy.72 = f32[8,15,10,2048]{3,2,1,0:T(8,128)} copy(f32[8,15,10,2048]{3,1,2,0:T(8,128)} %all-to-all-done) | data formatting | bytes 19660800 | tf_op jit(solution)/shard_map/reshape | solution.py:62
  181.7 15.0 %gather_fusion.1 = f32[120,10,2048]{2,1,0:T(8,128)} fusion(f32[120,10,2048]{2,1,0:T(8,128)} %bitcast.31, s32[1024]{0:T(1024)S(1)} %pad_clamp_fusion.1), kind=kCustom, calls=%fused_computation.1.clone | custom fusion | bytes 19661280 | tf_op jit(solution)/shard_map/jit(_take)/gather | solution.py:70
  196.7 15.3 %gather_fusion.3 = f32[120,10,2048]{2,1,0:T(8,128)} fusion(f32[120,10,2048]{2,1,0:T(8,128)} %bitcast.32, s32[1024]{0:T(1024)S(1)} %pad_clamp_fusion), kind=kCustom, calls=%fused_computation.3.clone | custom fusion | bytes 19661280 | tf_op jit(solution)/shard_map/jit(_take)/gather | solution.py:73
  212.0 12.8 %broadcast_select_fusion.1 = f32[120,10,2048]{2,1,0:T(8,128)} fusion(f32[120,10,2048]{2,1,0:T(8,128)} %gather_fusion.1, pred[120]{0:T(512)(128)(4,1)S(1)} %compare_and_fusion.1), kind=kLoop, calls=%fused_computation.17 | loop fusion | flops 2457600 | bytes 19660920 | tf_op jit(solution)/shard_map/jit(_take)/select_n | solution.py:70
  224.8 2.9 %copy-done = f32[120,10,2048]{2,1,0:T(8,128)S(1)} copy-done((f32[120,10,2048]{2,1,0:T(8,128)S(1)}, f32[120,10,2048]{2,1,0:T(8,128)}, u32[]{:S(2)}) %copy-start) | copy-done | bytes 9830424
  227.7 6.1 %broadcast_select_fusion = f32[120,10,2048]{2,1,0:T(8,128)} fusion(f32[120,10,2048]{2,1,0:T(8,128)S(1)} %copy-done, pred[120]{0:T(512)(128)(4,1)S(1)} %compare_and_fusion), kind=kLoop, calls=%fused_computation.16 | loop fusion | flops 2457600 | bytes 19660920 | tf_op jit(solution)/shard_map/jit(_take)/select_n | solution.py:73
  233.8 19.0 %fusion = f32[8,15,10,2048]{3,1,0,2:T(8,128)S(1)} fusion(f32[8,15,10,2048]{3,2,1,0:T(8,128)} %bitcast.34, f32[8,15,10,2048]{3,2,1,0:T(8,128)} %bitcast.33, f32[8,15]{1,0:T(8,128)S(1)} %bitcast_select_fusion, f32[8,15]{1,0:T(8,128)S(1)} %select_bitcast_fusion), kind=kLoop, calls=%fused_computation.6 | loop fusion | flops 7372800 | bytes 29492160 | tf_op jit(solution)/shard_map/add | solution.py:76
  252.8 5.5 %fusion.26 = (f32[8,15,8,2047]{3,1,0,2:T(8,128)S(1)}, f32[8,15,8,2047]{3,1,0,2:T(8,128)}) fusion(f32[8,15,10,2048]{3,1,0,2:T(8,128)S(1)} %fusion), kind=kLoop, calls=%fused_computation.78 | loop fusion | bytes 31441920 | tf_op jit(solution)/shard_map/slice | solution.py:23
  258.3 8.8 %fusion.5 = f32[15,8,2048]{2,0,1:T(8,128)S(1)} fusion(f32[8,15,10,2048]{3,1,0,2:T(8,128)S(1)} %fusion, f32[8,15,8,2047]{3,1,0,2:T(8,128)} %get-tuple-element.14, f32[8,15,8,2047]{3,1,0,2:T(8,128)S(1)} %get-tuple-element.13, f32[8,8,2048]{2,0,1:T(8,128)S(1)} %copy.70, f32[8,8,2048]{2,0,1:T(8,128)S(1)} %copy.69, f32[8,8,2048]{2,0,1:T(8,128)S(1)} %copy-done.2, ...), kind=kLoop, calls=%fused_computation.13 | loop fusion | flops 23347200 | bytes 42394112 | tf_op jit(solution)/shard_map/reduce_sum | solution.py:82
  267.1 1.6 copy_multiply_fusion.2
  (49 shorter events, 2.6 us)
Async XLA Ops:
  3.2 2.6 collective-permute-start
  4.5 5.6 %collective-permute-start.1 = (f32[23,1,2048]{2,0,1:T(8,128)S(1)}, f32[23,1,2048]{2,0,1:T(8,128)S(1)}, u32[]{:S(2)}, u32[]{:S(2)}) collective-permute-start(f32[23,1,2048]{2,0,1:T(8,128)S(1)} %get-tuple-element.18), channel_id=1, source_target_pairs={{1,0},{2,1},{3,2},{4,3},{5,4},{6,5},{7,6},{8,7},{9,8},{10,9},{11,1... | collective-permute-start | bytes 565256 | tf_op jit(solution)/shard_map/ppermute | solution.py:15
  10.1 5.4 %copy-start.3 = (f32[23,1,2048]{2,0,1:T(8,128)}, f32[23,1,2048]{2,0,1:T(8,128)S(1)}, u32[]{:S(2)}) copy-start(f32[23,1,2048]{2,0,1:T(8,128)S(1)} %collective-permute-done.1) | copy-start | bytes 565252
  15.5 7.1 %slice-start = ((s32[624,3]{0,1:T(4,128)}), s32[624,2]{0,1:T(2,128)S(1)}, s32[]{:S(2)}) async-start(s32[624,3]{0,1:T(4,128)} %param.11), calls=%async_computation.1 | async-start | bytes 10240 | tf_op jit(solution)/shard_map/slice | solution.py:28
  15.5 7.1 %copy-start.6 = (s32[120]{0:T(128)S(1)}, s32[120]{0:T(128)}, u32[]{:S(2)}) copy-start(s32[120]{0:T(128)} %param.13) | copy-start | bytes 1444
  15.5 7.3 %copy-start.4 = (s32[624,3]{0,1:T(4,128)S(1)}, s32[624,3]{0,1:T(4,128)}, u32[]{:S(2)}) copy-start(s32[624,3]{0,1:T(4,128)} %param.11) | copy-start | bytes 22468
  15.5 7.3 %copy-start.5 = (s32[624,2]{0,1:T(2,128)S(1)}, s32[624,2]{0,1:T(2,128)}, u32[]{:S(2)}) copy-start(s32[624,2]{0,1:T(2,128)} %param.12) | copy-start | bytes 14980
  15.5 150.2 %all-to-all-start = ((f32[8,15,10,2048]{3,1,2,0:T(8,128)}), f32[8,15,10,2048]{3,1,2,0:T(8,128)}, u32[]{:S(2)}, u32[]{:S(2)}) async-start(f32[8,15,10,2048]{3,1,2,0:T(8,128)} %stack.2), calls=%async_computation | async-start | bytes 20971520 | tf_op jit(solution)/shard_map/all_to_all | solution.py:63
  22.6 12.3 %copy-start.1 = (f32[8,8,2048]{2,1,0:T(8,128)S(1)}, f32[8,8,2048]{2,1,0:T(8,128)}, u32[]{:S(2)}) copy-start(f32[8,8,2048]{2,1,0:T(8,128)} %param.10) | copy-start | bytes 1572868
  212.0 15.7 %copy-start = (f32[120,10,2048]{2,1,0:T(8,128)S(1)}, f32[120,10,2048]{2,1,0:T(8,128)}, u32[]{:S(2)}) copy-start(f32[120,10,2048]{2,1,0:T(8,128)} %gather_fusion.3) | copy-start | bytes 29491204
  252.8 5.5 %copy-start.2 = (f32[8,8,2048]{2,0,1:T(8,128)S(1)}, f32[8,8,2048]{2,0,1:T(8,128)}, u32[]{:S(2)}) copy-start(f32[8,8,2048]{2,0,1:T(8,128)} %get-tuple-element.16) | copy-start | bytes 1572868
